TPU v7x, 256 devices: a whole 4x4x8 slice. The times are simulated.
256 devices in a mesh: seq: 16 (over z, core), head: 16 (over x, y).
Axes of the slice: x: 4, y: 4, z: 8, core: 2. Of those that a mesh axis runs over, the one named last changes fastest.
Arguments:
- hidden_in: bfloat16 [4, 128, 2048], P(None, None, 'seq'), may hold values from -6 to 6
- attn_gain: float32 [2048], P('seq'), may hold values from 0.1 to 1.9
- attn_router: bfloat16 [2048, 8], P('seq'), may hold values from -0.125 to 0.125
- query_weight: bfloat16 [2048, 8, 2048], P('seq', None, 'head'), may hold values from -0.125 to 0.125
- kv_weight: bfloat16 [2048, 4096], P('seq', 'head'), may hold values from -0.125 to 0.125
- out_weight: bfloat16 [8, 2048, 2048], P(None, 'head', 'seq'), may hold values from -0.09375 to 0.09375
- mlp_gain: float32 [2048], replicated, may hold values from 0.1 to 1.9
- mlp_router: bfloat16 [2048, 8], replicated, may hold values from -0.125 to 0.125
- gate_weight: bfloat16 [2048, 45056], P(None, ('seq', 'head')), may hold values from -0.125 to 0.125
- up_weight: bfloat16 [2048, 45056], P(None, ('seq', 'head')), may hold values from -0.125 to 0.125
- down_weight: bfloat16 [45056, 2048], P(('seq', 'head')), may hold values from -0.3125 to 0.3125
- cache: bfloat16 [196608, 4096], P('seq', 'head'), as said below
- token_req: int32 [196608], P('seq'), may hold values from -1 to 127, as said below
- attn_route: int32 [4, 128, 2], replicated, may hold values from 0 to 7, all different within a row
- mlp_route: int32 [4, 128, 2], replicated, may hold values from 0 to 7, all different within a row; in each aligned block of 512 rows (0 to 511, 512 to 1023, ..., all dimensions but the last counted through in order) at most 192 rows name the same one
- owner: int32 [128], replicated, may hold values from 0 to 15, as said below
Outputs:
- hidden_out: bfloat16 [4, 128, 2048], P(None, 'head', 'seq')
- new_cache: bfloat16 [160, 4, 4096], P('seq', None, 'head')
Inputs may be any that keep to these rules, and one draw needn't show every extreme that they name: `token_req`: slots form pages of 128; the live slots of a page belong to one request; request r has lengths[r] live slots; four requests have exactly 32768, every other at least one and less than 512. At most 10 requests share an owner, and some owner has exactly 10. `cache`: rows of empty slots hold values too. `attn_route`: the 2 experts of a token differ. `mlp_route`: the 2 experts of a token differ; over all 4 x 128 tokens no expert is chosen more than 192 times, and one is chosen exactly 192 times.
All inputs are finite; a program needn't handle non-finite values.
Results may differ from a plain program's by a relative error of at most 0.019.
Values may be sent and summed in bfloat16 or wider, within the bound.
No kernel may reach another device: no remote copies, remote signals or barrier semaphores. Data moves between devices by JAX's collectives and lax.ppermute only.
A program may use at most 64 MiB of HBM per device.

v0:
```python
import math
import jax
import jax.numpy as jnp
from jax import lax
from jax.sharding import PartitionSpec as P

D = 2048
HD = 128
FF = 5632
PAGE = 128
OWN_MAX = 10
epsilon = 1e-06
masked_score = -1e30


def frequency(width):
    return jnp.power(jnp.float32(10000.0), -2.0 * jnp.arange(width // 2, dtype=jnp.float32) / width)


def rotate(values, angles):
    half_width = values.shape[-1] // 2
    cosine = jnp.cos(angles)
    sine_part = jnp.sin(angles)
    lower_half = values[..., :half_width]
    upper_half = values[..., half_width:]
    return jnp.concatenate(
        [
            lower_half * cosine - upper_half * sine_part,
            upper_half * cosine + lower_half * sine_part,
        ],
        axis=-1,
    )


def on_device(
    hidden_in,
    attn_gain,
    attn_router,
    query_weight,
    kv_weight,
    out_weight,
    mlp_gain,
    mlp_router,
    gate_weight,
    up_weight,
    down_weight,
    cache,
    token_req,
    attn_route,
    mlp_route,
    owner,
):
    highest = lax.Precision.HIGHEST
    step_count, req_count, local_width = hidden_in.shape
    head_count = lax.axis_size("head")
    seq_index = lax.axis_index("seq")
    head_index = lax.axis_index("head")
    experts = query_weight.shape[1]
    heads_dev = kv_weight.shape[1] // (2 * HD)
    top_count = attn_route.shape[2]
    tok_rows = step_count * req_count
    queries_all = step_count * top_count
    hidden_f = hidden_in.astype(jnp.float32)
    squares = jnp.sum(hidden_f * hidden_f, axis=2)
    scaled = (hidden_f * attn_gain).astype(jnp.bfloat16).reshape(tok_rows, local_width)
    query_part = jnp.dot(
        scaled,
        query_weight.reshape(local_width, experts * heads_dev * HD),
        preferred_element_type=jnp.float32,
    ).reshape(step_count, req_count, experts, heads_dev * HD)
    kv_part = jnp.dot(scaled, kv_weight, preferred_element_type=jnp.float32).reshape(
        step_count, req_count, heads_dev * 2 * HD
    )
    logit_part = jnp.dot(scaled, attn_router, preferred_element_type=jnp.float32).reshape(
        step_count, req_count, experts
    )
    request_ids = jnp.arange(req_count, dtype=jnp.int32)
    counts = jnp.sum((token_req[:, None] == request_ids[None, :]).astype(jnp.float32), axis=0)
    attn_hot = (attn_route[..., None] == jnp.arange(experts, dtype=jnp.int32)).astype(jnp.float32)
    query_sum, kv_sum, logit_sum, square_sum, lengths = lax.psum(
        (query_part, kv_part, logit_part, squares, counts), "seq"
    )
    picked = jnp.einsum("srke,srec->srkc", attn_hot, query_sum, precision=highest)
    inverse = lax.rsqrt(square_sum / D + epsilon)
    attn_gates = jax.nn.softmax(
        jnp.sum(attn_hot * (logit_sum * inverse[..., None])[:, :, None, :], axis=3), axis=2
    )
    positions = lengths[None, :] + jnp.arange(step_count, dtype=jnp.float32)[:, None]
    freq_table = frequency(HD)
    queries = (picked * inverse[..., None, None]).reshape(
        step_count, req_count, top_count, heads_dev, HD
    )
    queries = rotate(queries, positions[:, :, None, None, None] * freq_table).astype(jnp.bfloat16)
    projected = kv_sum.reshape(step_count, req_count, heads_dev, 2 * HD) * inverse[..., None, None]
    new_keys = rotate(projected[..., :HD], positions[:, :, None, None] * freq_table).astype(
        jnp.bfloat16
    )
    new_values = projected[..., HD:].astype(jnp.bfloat16)
    new_rows = jnp.concatenate([new_keys, new_values], axis=3).reshape(
        step_count, req_count, heads_dev * 2 * HD
    )
    owned_flag = (owner == seq_index).astype(jnp.int32)
    before = (request_ids[None, :] < request_ids[:, None]).astype(jnp.int32)
    slot_rank = jnp.sum(before * owned_flag[None, :], axis=1)
    slot_ids = jnp.arange(OWN_MAX, dtype=jnp.int32)
    select = ((owned_flag[None, :] == 1) & (slot_rank[None, :] == slot_ids[:, None])).astype(
        jnp.bfloat16
    )
    appended = jnp.einsum(
        "jr,src->jsc", select, new_rows, preferred_element_type=jnp.float32
    ).astype(jnp.bfloat16)
    page_total = token_req.shape[0] // PAGE
    page_owner = token_req.reshape(page_total, PAGE)
    page_req = jnp.max(page_owner, axis=1)
    page_pick = jnp.maximum(page_req, 0)
    live_slot = page_owner >= 0
    req_hot = (page_req[None, :] == request_ids[:, None]).astype(jnp.float32)
    query_rows = jnp.transpose(queries, (1, 3, 0, 2, 4)).reshape(
        req_count, heads_dev, queries_all, HD
    )
    page_queries = query_rows[page_pick]
    paged = cache.reshape(page_total, PAGE, heads_dev, 2 * HD)
    score_scale = 1.0 / math.sqrt(HD)
    scores = (
        jnp.einsum(
            "phqd,pthd->phqt", page_queries, paged[..., :HD], preferred_element_type=jnp.float32
        )
        * score_scale
    )
    scores = jnp.where(live_slot[:, None, None, :], scores, masked_score)
    fresh_keys = jnp.transpose(new_keys, (1, 2, 0, 3))
    fresh_values = jnp.transpose(new_values, (1, 2, 0, 3))
    fresh_scores = (
        jnp.einsum("rhqd,rhsd->rhqs", query_rows, fresh_keys, preferred_element_type=jnp.float32)
        * score_scale
    )
    query_step = jnp.arange(queries_all) // top_count
    causal = jnp.arange(step_count)[None, :] <= query_step[:, None]
    fresh_live = causal[None, None, :, :] & (owned_flag[:, None, None, None] == 1)
    fresh_scores = jnp.where(fresh_live, fresh_scores, masked_score)
    page_best = jnp.max(scores, axis=3)
    local_best = jnp.max(
        jnp.where(req_hot[:, :, None, None] > 0, page_best[None], masked_score), axis=1
    )
    local_best = jnp.maximum(local_best, jnp.max(fresh_scores, axis=3))
    maxima = lax.pmax(local_best, "seq")
    page_probs = jnp.where(
        live_slot[:, None, None, :], jnp.exp(scores - maxima[page_pick][..., None]), 0.0
    )
    page_sums = jnp.sum(page_probs, axis=3)
    page_out = jnp.einsum(
        "phqt,pthd->phqd",
        page_probs.astype(jnp.bfloat16),
        paged[..., HD:],
        preferred_element_type=jnp.float32,
    )
    fresh_probs = jnp.where(fresh_live, jnp.exp(fresh_scores - maxima[..., None]), 0.0)
    totals = jnp.einsum("rp,phq->rhq", req_hot, page_sums, precision=highest) + jnp.sum(
        fresh_probs, axis=3
    )
    outputs = jnp.einsum("rp,phqd->rhqd", req_hot, page_out, precision=highest)
    outputs = outputs + jnp.einsum(
        "rhqs,rhsd->rhqd",
        fresh_probs.astype(jnp.bfloat16),
        fresh_values,
        preferred_element_type=jnp.float32,
    )
    local_totals = totals
    local_outputs = outputs
    totals, outputs = (
        lax.psum(local_totals.astype(jnp.bfloat16), "seq").astype(jnp.float32),
        lax.psum(local_outputs.astype(jnp.bfloat16), "seq").astype(jnp.float32),
    )
    attention = outputs / totals[..., None]
    attention = jnp.transpose(
        attention.reshape(req_count, heads_dev, step_count, top_count, HD), (2, 0, 3, 1, 4)
    )
    weighted = (attention * attn_gates[..., None, None]).astype(jnp.bfloat16)
    mixed = jnp.einsum(
        "srkhd,srke->srehd", weighted.astype(jnp.float32), attn_hot, precision=highest
    ).astype(jnp.bfloat16)
    head_part = jnp.dot(
        mixed.reshape(tok_rows, experts * heads_dev * HD),
        out_weight.reshape(experts * heads_dev * HD, local_width),
        preferred_element_type=jnp.float32,
    ).reshape(step_count, req_count, local_width)
    attn_out = lax.psum(head_part.astype(jnp.bfloat16), "head").astype(jnp.float32)
    residual = (hidden_f + attn_out).astype(jnp.bfloat16)
    full_rows = lax.all_gather(residual, "seq", axis=2, tiled=True)
    full_f = full_rows.astype(jnp.float32)
    inverse_mlp = lax.rsqrt(jnp.mean(full_f * full_f, axis=2) + epsilon)
    normed = (full_f * inverse_mlp[..., None] * mlp_gain).astype(jnp.bfloat16).reshape(tok_rows, D)
    mlp_logits = jnp.dot(normed, mlp_router, preferred_element_type=jnp.float32).reshape(
        step_count, req_count, experts
    )
    mlp_hot = (mlp_route[..., None] == jnp.arange(experts, dtype=jnp.int32)).astype(jnp.float32)
    mlp_gates = jax.nn.softmax(jnp.sum(mlp_hot * mlp_logits[:, :, None, :], axis=3), axis=2)
    combine_w = jnp.sum(mlp_hot * mlp_gates[..., None], axis=2)
    unit_count = gate_weight.shape[1]
    device_index = seq_index * head_count + head_index
    expert_index = device_index * unit_count // FF
    expert_ids = jnp.arange(experts, dtype=jnp.int32)
    rows_dev = req_count // head_count
    expert_weight = jnp.sum(
        combine_w * (expert_ids == expert_index).astype(jnp.float32), axis=2
    ).reshape(tok_rows, 1)
    gate_pre = jnp.dot(normed, gate_weight, preferred_element_type=jnp.float32)
    up_pre = jnp.dot(normed, up_weight, preferred_element_type=jnp.float32)
    hidden_units = (jax.nn.silu(gate_pre) * up_pre).astype(jnp.bfloat16)
    expert_term = (
        jnp.dot(hidden_units, down_weight, preferred_element_type=jnp.float32) * expert_weight
    ).reshape(step_count, req_count, D)
    by_columns = lax.psum_scatter(
        expert_term.astype(jnp.bfloat16), "seq", scatter_dimension=2, tiled=True
    )
    expert_part = lax.psum_scatter(by_columns, "head", scatter_dimension=1, tiled=True).astype(
        jnp.float32
    )
    own_rows = lax.dynamic_slice_in_dim(residual, head_index * rows_dev, rows_dev, 1)
    hidden_out = (own_rows.astype(jnp.float32) + expert_part).astype(jnp.bfloat16)
    return (hidden_out, appended)


def solution(mesh):
    in_specs = (
        P(None, None, "seq"),
        P("seq"),
        P("seq", None),
        P("seq", None, "head"),
        P("seq", "head"),
        P(None, "head", "seq"),
        P(),
        P(),
        P(None, ("seq", "head")),
        P(None, ("seq", "head")),
        P(("seq", "head"), None),
        P("seq", "head"),
        P("seq"),
        P(),
        P(),
        P(),
    )
    out_specs = (P(None, "head", "seq"), P("seq", None, "head"))
    return jax.shard_map(
        on_device, mesh=mesh, in_specs=in_specs, out_specs=out_specs, check_vma=False
    )
```

profile of v0, /device:TPU:2, one launch (start us, length us, event | category | flops | bytes accessed | tf_op | source)
XLA Modules:
  0.0 634.6 jit_solution(8452154288114500692)
XLA Ops:
  8.5 2.0 fusion.79
  10.4 2.7 fusion.67
  13.4 5.5 convert_reduce_fusion
  19.2 50.9 %all-reduce.1 = (f32[4,128]{1,0:T(4,128)S(1)}, f32[128]{0:T(128)S(1)}, f32[4,128,8]{1,2,0:T(8,128)S(1)}) all-reduce(f32[4,128]{1,0:T(4,128)S(1)} %fusion.46, f32[128]{0:T(128)S(1)} %convert_reduce_fusion, f32[4,128,8]{1,2,0:T(8,128)S(1)} %fusion.77), channel_id=1, replica_groups=mesh['seq'=16,'head'=16] {'seq'}, use_global_device_ids=true, to_apply=%region_3.0 | all-reduce | flops 4736 | bytes 37888 | tf_op jit(solution)/shard_map/psum | solution.py:80
  70.6 7.3 %select_reduce_fusion.2 = f32[4,128,2]{2,1,0:T(8,128)S(1)} fusion(f32[4,128,8]{2,1,0:T(8,128)S(1)} %copy.124, s32[4,128,2]{2,1,0:T(8,128)S(1)} %copy.111), kind=kLoop, calls=%fused_computation.46 | loop fusion | flops 23552 | bytes 24576 | tf_op jit(solution)/shard_map/reduce_sum | solution.py:86
  79.8 53.4 %all-reduce.14.cloned.1.call-done = (f32[4,128,256]{2,1,0:T(8,128)}, f32[4,128,8,128]{3,1,2,0:T(8,128)}) async-done(((f32[4,128,256]{2,1,0:T(8,128)}, f32[4,128,8,128]{3,1,2,0:T(8,128)}), (f32[4,128,256]{2,1,0:T(8,128)}, f32[4,128,8,128]{3,1,2,0:T(8,128)})) %all-reduce.14.cloned.1.call-update) | async-done | bytes 2621456 | tf_op jit(solution)/shard_map/psum | solution.py:80
  133.2 1.3 multiply_bitcast_fusion
  134.5 1.2 fusion.42
  135.8 3.2 fusion.12
  141.4 3.7 fusion.101
  146.0 48.3 %pmax.7 = f32[128,1,8]{2,0,1:T(8,128)S(1)} all-reduce(f32[128,1,8]{2,0,1:T(8,128)S(1)} %maximum_bitcast_fusion.4), channel_id=1, replica_groups=mesh['seq'=16,'head'=16] {'seq'}, use_global_device_ids=true, to_apply=%region_10.0 | all-reduce | flops 1024 | bytes 8192 | tf_op jit(solution)/shard_map/pmax | solution.py:146
  194.9 2.9 fusion.5
  199.1 1.3 fusion.21
  200.7 23.6 %psum.61 = bf16[128,8]{0,1:T(8,128)(2,1)S(1)} all-reduce(bf16[128,8]{0,1:T(8,128)(2,1)S(1)} %fusion.26), channel_id=1, replica_groups=mesh['seq'=16,'head'=16] {'seq'}, use_global_device_ids=true, to_apply=%region_14.15 | all-reduce | flops 1024 | bytes 4096 | tf_op jit(solution)/shard_map/psum | solution.py:171
  224.3 83.3 %all-reduce.8.cloned.1.call-done = bf16[128,1,8,128]{3,0,2,1:T(8,128)(2,1)} async-done(((bf16[128,1,8,128]{3,0,2,1:T(8,128)(2,1)}), bf16[128,1,8,128]{3,0,2,1:T(8,128)(2,1)}) %all-reduce.8.cloned.1.call-update) | async-done | bytes 262160 | tf_op jit(solution)/shard_map/psum | solution.py:172
  307.6 1.2 convert_divide_fusion
  308.8 2.7 convolution_convert_fusion
  311.6 1.1 fusion.25
  312.7 92.5 %all-reduce.10.cloned.1.call-done = bf16[4,128,128]{2,1,0:T(8,128)(2,1)} async-done(((bf16[4,128,128]{2,1,0:T(8,128)(2,1)}), bf16[4,128,128]{2,1,0:T(8,128)(2,1)}) %all-reduce.10.cloned.1.call-update) | async-done | bytes 131088 | tf_op jit(solution)/shard_map/psum | solution.py:187
  405.2 1.6 fusion.47
  407.1 40.6 %all-gather.2.cloned.1.call-done = bf16[4,128,2048]{2,1,0:T(8,128)(2,1)} async-done(((bf16[4,128,128]{2,1,0:T(8,128)(2,1)}), bf16[4,128,2048]{2,1,0:T(8,128)(2,1)}) %all-gather.2.cloned.1.call-update) | async-done | bytes 2097168 | tf_op jit(solution)/shard_map/all_gather | solution.py:189
  447.7 2.2 fusion.2
  450.5 1.3 copy-done.2
  452.6 7.3 %select_reduce_fusion.1 = f32[4,128,2]{2,1,0:T(8,128)S(1)} fusion(f32[4,128,8]{2,1,0:T(8,128)S(1)} %fusion.85, s32[4,128,2]{2,1,0:T(8,128)S(1)} %copy.126), kind=kLoop, calls=%fused_computation.44 | loop fusion | flops 23552 | bytes 24576 | tf_op jit(solution)/shard_map/reduce_sum | solution.py:197
  460.1 1.4 select_reduce_fusion
  461.7 3.5 fusion.104
  465.2 4.1 multiply_convert_fusion
  469.4 3.1 copy.133
  472.5 1.7 copy.166
  476.2 56.6 %reduce-scatter.5.cloned.1.call-done = bf16[128,512]{1,0:T(8,128)(2,1)} async-done(((bf16[2048,512]{1,0:T(8,128)(2,1)}), bf16[128,512]{1,0:T(8,128)(2,1)}) %reduce-scatter.5.cloned.1.call-update) | async-done | bytes 131088
  535.5 91.0 %all-reduce.12.cloned.1.call-done = bf16[4,128,128]{2,1,0:T(8,128)(2,1)} async-done(((bf16[4,128,128]{2,1,0:T(8,128)(2,1)}), bf16[4,128,128]{2,1,0:T(8,128)(2,1)}) %all-reduce.12.cloned.1.call-update) | async-done | bytes 131088
  626.5 1.3 add_convert_fusion.1
  (100 shorter events, 15.6 us)
Async XLA Ops:
  7.2 458.1 %copy-start = (bf16[176,2048]{1,0:T(8,128)(2,1)S(1)}, bf16[176,2048]{1,0:T(8,128)(2,1)}, u32[]{:S(2)}) copy-start(bf16[176,2048]{1,0:T(8,128)(2,1)} %param.26) | copy-start | bytes 2162692
  7.2 126.0 %all-reduce.14.cloned.1.call-start = ((), (), s32[]{:S(2)}) async-start(), calls=%async_computation.6 | async-start | bytes 5242880 | tf_op jit(solution)/shard_map/psum | solution.py:80
  10.4 2.8 copy-start.4
  10.4 3.0 copy-start.7
  10.4 8.7 %copy-start.11 = (f32[128]{0:T(128)S(1)}, f32[128]{0:T(128)}, u32[]{:S(2)}) copy-start(f32[128]{0:T(128)} %param.17) | copy-start | bytes 1540
  10.4 8.7 %copy-start.16 = (bf16[128,8]{0,1:T(8,128)(2,1)S(1)}, bf16[128,8]{0,1:T(8,128)(2,1)}, u32[]{:S(2)}) copy-start(bf16[128,8]{0,1:T(8,128)(2,1)} %param.18) | copy-start | bytes 6148
  13.1 57.1 %copy-start.12 = (s32[128]{0:T(128)S(1)}, s32[128]{0:T(128)}, u32[]{:S(2)}) copy-start(s32[128]{0:T(128)} %param.31) | copy-start | bytes 1540
  13.1 57.1 %copy-start.9 = (s32[4,128,2]{1,2,0:T(2,128)S(1)}, s32[4,128,2]{1,2,0:T(2,128)}, u32[]{:S(2)}) copy-start(s32[4,128,2]{1,2,0:T(2,128)} %param.29) | copy-start | bytes 12292
  13.2 294.5 %all-reduce.8.cloned.1.call-start = ((), (), s32[]{:S(2)}) async-start(), calls=%async_computation.1 | async-start | bytes 524288 | tf_op jit(solution)/shard_map/psum | solution.py:172
  133.2 2.6 copy-start.13
  135.7 9.7 %copy-start.5 = (bf16[4,128,1,64]{3,1,0,2:T(8,128)(2,1)}, bf16[4,128,1,64]{3,1,0,2:T(8,128)(2,1)S(1)}, u32[]{:S(2)}) copy-start(bf16[4,128,1,64]{3,1,0,2:T(8,128)(2,1)S(1)} %get-tuple-element.26) | copy-start | bytes 196612
  200.4 204.9 %all-reduce.10.cloned.1.call-start = ((), (), s32[]{:S(2)}) async-start(), calls=%async_computation.2 | async-start | bytes 262144 | tf_op jit(solution)/shard_map/psum | solution.py:187
  308.8 2.7 copy-start.14
  311.5 95.4 %copy-start.10 = (s32[4,128,2]{1,2,0:T(2,128)S(1)}, s32[4,128,2]{1,2,0:T(2,128)}, u32[]{:S(2)}) copy-start(s32[4,128,2]{1,2,0:T(2,128)} %param.30) | copy-start | bytes 12292
  311.6 138.4 %copy-start.8 = (f32[2048]{0:T(1024)S(1)}, f32[2048]{0:T(1024)}, u32[]{:S(2)}) copy-start(f32[2048]{0:T(1024)} %param.22) | copy-start | bytes 24580
  312.7 135.0 %all-gather.2.cloned.1.call-start = ((), (), s32[]{:S(2)}) async-start(), calls=%async_computation.3 | async-start | bytes 2228224 | tf_op jit(solution)/shard_map/all_gather | solution.py:189
  406.8 126.0 %reduce-scatter.5.cloned.1.call-start = ((), (), s32[]{:S(2)}) async-start(), calls=%async_computation.4 | async-start | bytes 2228224
  447.7 2.2 copy-start.1
  450.0 1.9 copy-start.15
  450.5 1.4 copy-start.2
  461.7 3.5 copy-start.3
  474.2 0.7 copy-start.17
  474.2 60.4 %copy-start.6 = (bf16[4,128,1,64]{3,1,0,2:T(8,128)(2,1)S(1)}, bf16[4,128,1,64]{3,1,0,2:T(8,128)(2,1)}, u32[]{:S(2)}) copy-start(bf16[4,128,1,64]{3,1,0,2:T(8,128)(2,1)} %copy-done.5) | copy-start | bytes 196612
  474.2 152.2 %all-reduce.12.cloned.1.call-start = ((), (), s32[]{:S(2)}) async-start(), calls=%async_computation.5 | async-start | bytes 262144
Sparse Core Ops, SparseCore 0:
  13.3 119.8 all-reduce.13
  200.5 107.0 all-reduce.7
  312.8 92.3 all-reduce.9
  407.0 40.6 all-gather.1
  474.3 58.4 reduce-scatter.4
  535.9 90.5 all-reduce.11
where the time goes:
time: 635 us
  waiting for transfers between devices  418 us (66%)
  blocking collectives  123 us (19%)
  other arithmetic  36 us (6%)
  matrix products  29.6 us (5%)
  between operations  15.3 us (2%)
  local copies, waits for them, and re-layouts  13.2 us (2%)
    unnamed x8, waiting for transfers between devices  148 us
    psum x1, waiting for transfers between devices, on_device(): lax.psum(head_part.astype(jnp.bfloat16), 'head').astype(jnp.float32)  92.5 us
    psum x1, waiting for transfers between devices, on_device(): lax.psum(local_outputs.astype(jnp.bfloat16), 'seq').astype(jnp.float32)  83.3 us
    psum x1, waiting for transfers between devices, on_device(): lax.psum((query_part, kv_part, logit_part, squares, counts), 'seq')  53.4 us
    psum x1, blocking collectives, on_device(): lax.psum((query_part, kv_part, logit_part, squares, counts), 'seq')  50.9 us
    pmax x1, blocking collectives, on_device(): maxima = lax.pmax(local_best, 'seq')  48.3 us
    all_gather x1, waiting for transfers between devices, on_device(): full_rows = lax.all_gather(residual, 'seq', axis=2, tiled=True)  40.6 us
    psum x1, blocking collectives, on_device(): lax.psum(local_totals.astype(jnp.bfloat16), 'seq').astype(jnp.float32)  23.6 us
  transfers between devices with their start and end apart: 6, of which 6 were waited for; matrix products, arithmetic and copies ran while one was open for 3% of the time, Pallas kernels for 0%

commit v1 on v0

--- a/solution.py
+++ b/solution.py
@@ -1,3 +1,4 @@
+import functools
 import math
 import jax
 import jax.numpy as jnp
@@ -11,6 +12,36 @@
 OWN_MAX = 10
 epsilon = 1e-06
 masked_score = -1e30
+
+
+def answer_the_things(q_in, join_dim):
+    q_in = jnp.moveaxis(q_in, 0, join_dim)
+    v_next = q_in.shape
+    return q_in.reshape(
+        *v_next[:join_dim], v_next[join_dim] * v_next[join_dim + 1], *v_next[join_dim + 2 :]
+    )
+
+
+def _watch_signs(panel, lane_axis, along_dim):
+    n_peers_all = lax.axis_size(lane_axis)
+    lanes = [(ii, (ii + 1) % n_peers_all) for ii in range(n_peers_all)]
+    slots = [(to_i, dev_i) for dev_i, to_i in lanes]
+    t1, carry_out = ([], [])
+    for u in range(n_peers_all - 1):
+        if u % 2 == 0:
+            mat_out = lax.ppermute(t1[-1] if t1 else panel, lane_axis, lanes)
+            t1.append(mat_out)
+        else:
+            outer = lax.ppermute(carry_out[-1] if carry_out else panel, lane_axis, slots)
+            carry_out.append(outer)
+    step_out = jnp.stack([*t1[::-1], panel, *carry_out])
+    piece_next = lax.axis_index(lane_axis)
+    after = piece_next - len(t1)
+    step_out = step_out[(jnp.arange(n_peers_all) - after) % n_peers_all]
+    return answer_the_things(step_out, along_dim)
+
+
+enter_the_orders = functools.partial(_watch_signs, lane_axis="seq", along_dim=2)
 
 
 def frequency(width):
@@ -186,7 +217,7 @@
     ).reshape(step_count, req_count, local_width)
     attn_out = lax.psum(head_part.astype(jnp.bfloat16), "head").astype(jnp.float32)
     residual = (hidden_f + attn_out).astype(jnp.bfloat16)
-    full_rows = lax.all_gather(residual, "seq", axis=2, tiled=True)
+    full_rows = enter_the_orders(residual)
     full_f = full_rows.astype(jnp.float32)
     inverse_mlp = lax.rsqrt(jnp.mean(full_f * full_f, axis=2) + epsilon)
     normed = (full_f * inverse_mlp[..., None] * mlp_gain).astype(jnp.bfloat16).reshape(tok_rows, D)

time: 635 us -> 666 us (1.049)
  local copies, waits for them, and re-layouts: 13.2 us -> 38.1 us
  starting transfers between devices: 0.25 us -> 20.9 us
  waiting for transfers between devices: 418 us -> 401 us
    all_gather x1 -> x0, waiting for transfers between devices: 40.6 us -> none  [on_device(): full_rows = lax.all_gather(residual, 'seq', axis=2, tiled=True)]
    ppermute x0 -> x15, waiting for transfers between devices: none -> 23.2 us  [the longest x8 23.2 us: _watch_signs(): mat_out = lax.ppermute(t1[-1] if t1 else panel, lane_axis, lanes)]
    ppermute x0 -> x15, starting transfers between devices: none -> 20.7 us  [the longest x7 20.7 us: _watch_signs(): lax.ppermute(carry_out[-1] if carry_out else panel, lane_axis, slots)]
    convert_element_type x0 -> x2, local copies, waits for them, and re-layouts: none -> 12.1 us  [on_device(): full_f = full_rows.astype(jnp.float32)]
    unnamed x45 -> x64, local copies, waits for them, and re-layouts: 11.1 us -> 20.8 us
    unnamed x8 -> x7, waiting for transfers between devices: 148 us -> 148 us
  transfers between devices with their start and end apart: 6 -> 20, of which waited for: 6 -> 13; matrix products, arithmetic and copies ran while one was open for 3% -> 4% of each run, Pallas kernels for 0% -> 0%
where the time goes in v1:
time: 666 us; the launch traced here: 665 us
  waiting for transfers between devices  401 us (60%)
  blocking collectives  123 us (18%)
  other arithmetic  40.2 us (6%)
  local copies, waits for them, and re-layouts  38.1 us (6%)
  matrix products  27.7 us (4%)
  starting transfers between devices  20.9 us (3%)
  between operations  14.9 us (2%)
    unnamed x7, waiting for transfers between devices  148 us
    psum x1, waiting for transfers between devices, on_device(): lax.psum(head_part.astype(jnp.bfloat16), 'head').astype(jnp.float32)  92.5 us
    psum x1, waiting for transfers between devices, on_device(): lax.psum(local_outputs.astype(jnp.bfloat16), 'seq').astype(jnp.float32)  83.4 us
    psum x1, waiting for transfers between devices, on_device(): lax.psum((query_part, kv_part, logit_part, squares, counts), 'seq')  53.4 us
    psum x1, blocking collectives, on_device(): lax.psum((query_part, kv_part, logit_part, squares, counts), 'seq')  50.9 us
    pmax x1, blocking collectives, on_device(): maxima = lax.pmax(local_best, 'seq')  48.3 us
    psum x1, blocking collectives, on_device(): lax.psum(local_totals.astype(jnp.bfloat16), 'seq').astype(jnp.float32)  23.6 us
    ppermute x8, waiting for transfers between devices, _watch_signs(): mat_out = lax.ppermute(t1[-1] if t1 else panel, lane_axis, lanes)  23.2 us
  transfers between devices with their start and end apart: 20, of which 13 were waited for; matrix products, arithmetic and copies ran while one was open for 4% of the time, Pallas kernels for 0%

profile of v1, /device:TPU:2, one launch (start us, length us, event | category | flops | bytes accessed | tf_op | source)
XLA Modules:
  0.0 665.4 jit_solution(17527002563581688016)
XLA Ops:
  10.4 2.7 fusion.69
  13.3 5.5 convert_reduce_fusion
  19.3 50.9 %all-reduce.1 = (f32[4,128]{1,0:T(4,128)S(1)}, f32[128]{0:T(128)S(1)}, f32[4,128,8]{1,2,0:T(8,128)S(1)}) all-reduce(f32[4,128]{1,0:T(4,128)S(1)} %fusion.48, f32[128]{0:T(128)S(1)} %convert_reduce_fusion, f32[4,128,8]{1,2,0:T(8,128)S(1)} %fusion.79), channel_id=1, replica_groups=mesh['seq'=16,'head'=16] {'seq'}, use_global_device_ids=true, to_apply=%region_3.0 | all-reduce | flops 4736 | bytes 37888 | tf_op jit(solution)/shard_map/psum | solution.py:111
  70.5 7.3 %select_reduce_fusion.2 = f32[4,128,2]{2,1,0:T(8,128)S(1)} fusion(f32[4,128,8]{2,1,0:T(8,128)S(1)} %copy.139, s32[4,128,2]{2,1,0:T(8,128)S(1)} %copy.126), kind=kLoop, calls=%fused_computation.51 | loop fusion | flops 23552 | bytes 24576 | tf_op jit(solution)/shard_map/reduce_sum | solution.py:117
  79.7 53.4 %all-reduce.14.cloned.1.call-done = (f32[4,128,256]{2,1,0:T(8,128)}, f32[4,128,8,128]{3,1,2,0:T(8,128)}) async-done(((f32[4,128,256]{2,1,0:T(8,128)}, f32[4,128,8,128]{3,1,2,0:T(8,128)}), (f32[4,128,256]{2,1,0:T(8,128)}, f32[4,128,8,128]{3,1,2,0:T(8,128)})) %all-reduce.14.cloned.1.call-update) | async-done | bytes 2621456 | tf_op jit(solution)/shard_map/psum | solution.py:111
  135.8 3.2 fusion.14
  141.4 3.7 fusion.106
  146.0 48.3 %pmax.7 = f32[128,1,8]{2,0,1:T(8,128)S(1)} all-reduce(f32[128,1,8]{2,0,1:T(8,128)S(1)} %maximum_bitcast_fusion.4), channel_id=1, replica_groups=mesh['seq'=16,'head'=16] {'seq'}, use_global_device_ids=true, to_apply=%region_10.0 | all-reduce | flops 1024 | bytes 8192 | tf_op jit(solution)/shard_map/pmax | solution.py:177
  195.2 2.9 fusion.7
  200.7 23.6 %psum.61 = bf16[128,8]{0,1:T(8,128)(2,1)S(1)} all-reduce(bf16[128,8]{0,1:T(8,128)(2,1)S(1)} %fusion.28), channel_id=1, replica_groups=mesh['seq'=16,'head'=16] {'seq'}, use_global_device_ids=true, to_apply=%region_14.15 | all-reduce | flops 1024 | bytes 4096 | tf_op jit(solution)/shard_map/psum | solution.py:202
  224.3 83.4 %all-reduce.8.cloned.1.call-done = bf16[128,1,8,128]{3,0,2,1:T(8,128)(2,1)} async-done(((bf16[128,1,8,128]{3,0,2,1:T(8,128)(2,1)}), bf16[128,1,8,128]{3,0,2,1:T(8,128)(2,1)}) %all-reduce.8.cloned.1.call-update) | async-done | bytes 262160 | tf_op jit(solution)/shard_map/psum | solution.py:203
  308.8 2.7 convolution_convert_fusion
  312.7 92.5 %all-reduce.10.cloned.1.call-done = bf16[4,128,128]{2,1,0:T(8,128)(2,1)} async-done(((bf16[4,128,128]{2,1,0:T(8,128)(2,1)}), bf16[4,128,128]{2,1,0:T(8,128)(2,1)}) %all-reduce.10.cloned.1.call-update) | async-done | bytes 131088 | tf_op jit(solution)/shard_map/psum | solution.py:218
  406.2 5.6 collective-permute-done
  411.8 3.0 collective-permute-start.8
  414.8 2.6 collective-permute-done.1
  417.4 3.0 collective-permute-start.9
  423.0 3.0 collective-permute-start.10
  426.0 2.6 collective-permute-done.3
  428.6 3.0 collective-permute-start.11
  434.3 3.0 collective-permute-start.12
  437.2 2.6 collective-permute-done.5
  439.9 3.0 collective-permute-start.13
  446.4 3.0 collective-permute-start.14
  467.1 5.4 copy.143
  472.5 6.7 %copy.141 = f32[4,128,16,128]{3,2,1,0:T(8,128)} copy(f32[4,128,16,128]{3,1,0,2:T(8,128)} %convert_bitcast_fusion) | data formatting | bytes 8388608 | tf_op jit(solution)/shard_map/convert_element_type | solution.py:221
  480.9 7.3 %select_reduce_fusion.1 = f32[4,128,2]{2,1,0:T(8,128)S(1)} fusion(f32[4,128,8]{2,1,0:T(8,128)S(1)} %fusion.87, s32[4,128,2]{2,1,0:T(8,128)S(1)} %copy-done.2), kind=kLoop, calls=%fused_computation.49 | loop fusion | flops 23552 | bytes 24576 | tf_op jit(solution)/shard_map/reduce_sum | solution.py:228
  490.0 4.1 fusion.4
  495.8 4.2 multiply_convert_fusion
  499.9 3.1 copy.152
  506.8 57.2 %reduce-scatter.5.cloned.1.call-done = bf16[128,512]{1,0:T(8,128)(2,1)} async-done(((bf16[2048,512]{1,0:T(8,128)(2,1)}), bf16[128,512]{1,0:T(8,128)(2,1)}) %reduce-scatter.5.cloned.1.call-update) | async-done | bytes 131088
  566.6 90.9 %all-reduce.12.cloned.1.call-done = bf16[4,128,128]{2,1,0:T(8,128)(2,1)} async-done(((bf16[4,128,128]{2,1,0:T(8,128)(2,1)}), bf16[4,128,128]{2,1,0:T(8,128)(2,1)}) %all-reduce.12.cloned.1.call-update) | async-done | bytes 131088
  (154 shorter events, 57.5 us)
Async XLA Ops:
  7.2 488.6 %copy-start = (bf16[176,2048]{1,0:T(8,128)(2,1)S(1)}, bf16[176,2048]{1,0:T(8,128)(2,1)}, u32[]{:S(2)}) copy-start(bf16[176,2048]{1,0:T(8,128)(2,1)} %param.26) | copy-start | bytes 2162692
  7.2 126.0 %all-reduce.14.cloned.1.call-start = ((), (), s32[]{:S(2)}) async-start(), calls=%async_computation.5 | async-start | bytes 5242880 | tf_op jit(solution)/shard_map/psum | solution.py:111
  10.4 8.4 %copy-start.3 = (bf16[4,128,128]{2,1,0:T(8,128)(2,1)S(1)}, bf16[4,128,128]{2,1,0:T(8,128)(2,1)}, u32[]{:S(2)}) copy-start(bf16[4,128,128]{2,1,0:T(8,128)(2,1)} %param.16) | copy-start | bytes 393220
  10.4 8.7 %copy-start.12 = (f32[128]{0:T(128)S(1)}, f32[128]{0:T(128)}, u32[]{:S(2)}) copy-start(f32[128]{0:T(128)} %param.17) | copy-start | bytes 1540
  10.4 8.7 %copy-start.18 = (bf16[128,8]{0,1:T(8,128)(2,1)S(1)}, bf16[128,8]{0,1:T(8,128)(2,1)}, u32[]{:S(2)}) copy-start(bf16[128,8]{0,1:T(8,128)(2,1)} %param.18) | copy-start | bytes 6148
  13.1 57.2 %copy-start.10 = (s32[4,128,2]{1,2,0:T(2,128)S(1)}, s32[4,128,2]{1,2,0:T(2,128)}, u32[]{:S(2)}) copy-start(s32[4,128,2]{1,2,0:T(2,128)} %param.29) | copy-start | bytes 12292
  13.2 294.5 %all-reduce.8.cloned.1.call-start = ((), (), s32[]{:S(2)}) async-start(), calls=%async_computation.1 | async-start | bytes 524288 | tf_op jit(solution)/shard_map/psum | solution.py:203
  135.7 9.6 %copy-start.4 = (bf16[4,128,1,64]{3,1,0,2:T(8,128)(2,1)}, bf16[4,128,1,64]{3,1,0,2:T(8,128)(2,1)S(1)}, u32[]{:S(2)}) copy-start(bf16[4,128,1,64]{3,1,0,2:T(8,128)(2,1)S(1)} %get-tuple-element.25) | copy-start | bytes 196612
  135.7 9.6 %copy-start.6 = (bf16[4,128,1,64]{3,1,0,2:T(8,128)(2,1)}, bf16[4,128,1,64]{3,1,0,2:T(8,128)(2,1)S(1)}, u32[]{:S(2)}) copy-start(bf16[4,128,1,64]{3,1,0,2:T(8,128)(2,1)S(1)} %get-tuple-element.26) | copy-start | bytes 196612
  200.4 204.8 %all-reduce.10.cloned.1.call-start = ((), (), s32[]{:S(2)}) async-start(), calls=%async_computation.2 | async-start | bytes 262144 | tf_op jit(solution)/shard_map/psum | solution.py:218
  311.6 133.9 %copy-start.11 = (s32[4,128,2]{1,2,0:T(2,128)S(1)}, s32[4,128,2]{1,2,0:T(2,128)}, u32[]{:S(2)}) copy-start(s32[4,128,2]{1,2,0:T(2,128)} %param.30) | copy-start | bytes 12292
  312.7 251.3 %reduce-scatter.5.cloned.1.call-start = ((), (), s32[]{:S(2)}) async-start(), calls=%async_computation.3 | async-start | bytes 2228224
  406.2 5.6 collective-permute-start
  411.8 5.6 collective-permute-start.1
  411.8 5.6 collective-permute-start.8
  417.4 5.6 collective-permute-start.2
  417.4 5.6 collective-permute-start.9
  423.0 5.6 collective-permute-start.3
  423.0 5.6 collective-permute-start.10
  428.6 5.6 collective-permute-start.4
  428.6 5.6 collective-permute-start.11
  434.2 5.6 collective-permute-start.5
  434.3 5.6 collective-permute-start.12
  439.8 5.6 collective-permute-start.6
  439.9 6.5 collective-permute-start.13
  445.5 5.6 collective-permute-start.7
  446.4 14.6 %collective-permute-start.14 = (bf16[4,128,128]{2,1,0:T(8,128)(2,1)S(1)}, bf16[4,128,128]{2,1,0:T(8,128)(2,1)S(1)}, u32[]{:S(2)}, u32[]{:S(2)}) collective-permute-start(bf16[4,128,128]{2,1,0:T(8,128)(2,1)S(1)} %collective-permute-done.13), channel_id=1, source_target_pairs={{16,0},{32,16},{48,32},{64,48},{80,64},{96,80},{112,96},{128,112},... | collective-permute-start | bytes 393224 | tf_op jit(solution)/shard_map/ppermute | solution.py:35
  472.5 6.7 %copy-start.1 = (f32[4,128,16,128]{1,3,2,0:T(8,128)S(1)}, f32[4,128,16,128]{1,3,2,0:T(8,128)}, u32[]{:S(2)}) copy-start(f32[4,128,16,128]{1,3,2,0:T(8,128)} %copy.143) | copy-start | bytes 12582916
  472.5 6.7 %copy-start.9 = (f32[2048]{0:T(1024)S(1)}, f32[2048]{0:T(1024)}, u32[]{:S(2)}) copy-start(f32[2048]{0:T(1024)} %param.22) | copy-start | bytes 24580
  504.7 61.0 %copy-start.5 = (bf16[4,128,1,64]{3,1,0,2:T(8,128)(2,1)S(1)}, bf16[4,128,1,64]{3,1,0,2:T(8,128)(2,1)}, u32[]{:S(2)}) copy-start(bf16[4,128,1,64]{3,1,0,2:T(8,128)(2,1)} %copy-done.4) | copy-start | bytes 196612
  504.7 61.0 %copy-start.7 = (bf16[4,128,1,64]{3,1,0,2:T(8,128)(2,1)S(1)}, bf16[4,128,1,64]{3,1,0,2:T(8,128)(2,1)}, u32[]{:S(2)}) copy-start(bf16[4,128,1,64]{3,1,0,2:T(8,128)(2,1)} %copy-done.6) | copy-start | bytes 196612
  504.8 152.8 %all-reduce.12.cloned.1.call-start = ((), (), s32[]{:S(2)}) async-start(), calls=%async_computation.4 | async-start | bytes 262144
  (8 other events, 20.7 us)
Sparse Core Ops, SparseCore 0:
  13.3 119.8 all-reduce.13
  200.6 107.0 all-reduce.7
  312.8 92.4 all-reduce.9
  504.9 59.0 reduce-scatter.4
  567.0 90.4 all-reduce.11
